TPU v7x, 32 devices: a whole 2x2x4 slice. The times are simulated.
32 devices in a mesh: dp: 2 (over x), mp: 16 (over z, y, core).
Axes of the slice: x: 2, y: 2, z: 4, core: 2. Of those that a mesh axis runs over, the one named last changes fastest.
Arguments:
- node_features: bfloat16 [512, 6144], P('mp', 'dp'), may hold values from -6 to 6
- weights_one: bfloat16 [1024, 512], replicated, may hold values from -0.25 to 0.25
- weights_two: bfloat16 [1024, 512], replicated, may hold values from -0.25 to 0.25
- neighbor_owner: int32 [6144, 8], P('dp'), may hold values from 0 to 15, all different within a row; in each aligned block of 192 rows (0 to 191, 192 to 383, ...) at most 144 rows name the same one
- neighbor_row: int32 [6144, 8], P('dp'), may hold values from 0 to 191
- neighbor_count: int32 [6144], P('dp'), may hold values from 4 to 8
- cotangent: bfloat16 [6144, 512], P(('dp', 'mp')), may hold values from -0.076171875 to 0.076171875
Outputs:
- node_output: bfloat16 [6144, 512], P(('dp', 'mp'))
- weight_grads: float32 [2048, 512], P(('dp', 'mp'))
Inputs may be any that keep to these rules, and one draw needn't show every extreme that they name: `neighbor_owner`: each row names 8 different owners; among the rows of one device (aligned blocks of 192 rows) no owner is named more than 144 times, and in some block one owner exactly 144 times. Slots k >= neighbor_count[r] are padding and carry no edge.
All inputs are finite; a program needn't handle non-finite values.
Results may differ from a plain program's by a relative error of at most 0.0052.
Values may be sent and summed in bfloat16 or wider, within the bound.
No kernel may reach another device: no remote copies, remote signals or barrier semaphores. Data moves between devices by JAX's collectives and lax.ppermute only.
A program may use at most 64 MiB of HBM per device.

v0:
```python
import jax
import jax.numpy as jnp
from jax import lax
from jax.sharding import PartitionSpec as P


def column_mean(table, indices, live, inverse):
    total = jnp.zeros((table.shape[0], indices.shape[1]), jnp.float32)
    for slot_index in range(indices.shape[0]):
        picked = jnp.take(table, indices[slot_index], axis=1)
        kept = jnp.where(live[slot_index][None, :], picked, jnp.zeros_like(picked))
        total = total + kept.astype(jnp.float32)
    return (total * inverse[None, :]).astype(jnp.bfloat16)


def silu_slope(values):
    sigmoid = jax.nn.sigmoid(values)
    return sigmoid * (1.0 + values * (1.0 - sigmoid))


def contract(left, right, left_dim, right_dim):
    return lax.dot_general(
        left, right, (((left_dim,), (right_dim,)), ((), ())), preferred_element_type=jnp.float32
    )


def shards(
    node_features, weights_one, weights_two, neighbor_owner, neighbor_row, neighbor_count, cotangent
):
    devices = lax.axis_size("mp")
    own_index = lax.axis_index("mp")
    node_dev = cotangent.shape[0]
    all_nodes = neighbor_owner.shape[0]
    fanout = neighbor_owner.shape[1]
    feat_width = weights_one.shape[0] // 2
    hidden = weights_one.shape[1]
    capacity = 3 * node_dev * fanout // (2 * devices)
    live = lax.broadcasted_iota(jnp.int32, (all_nodes, fanout), 1) < neighbor_count[:, None]
    inverse_all = 1.0 / neighbor_count.astype(jnp.float32)
    owner_ids = lax.broadcasted_iota(jnp.int32, (devices, 1, 1), 0)
    match = (neighbor_owner[None, :, :] == owner_ids) & live[None, :, :]
    rowsel = jnp.max(jnp.where(match, neighbor_row[None, :, :], -1), axis=2)
    has = rowsel >= 0
    with jax.named_scope("layer_one_mean"):
        if all_nodes * all_nodes <= 4096 * 4096:
            row_ids = lax.broadcasted_iota(jnp.int32, (1, node_dev, 1), 1)
            adjacency = (rowsel[:, None, :] == row_ids).astype(jnp.bfloat16)
            adjacency = adjacency.reshape(devices * node_dev, all_nodes)
            summed = contract(node_features, adjacency, 1, 0)
            agg_one_cols = (summed * inverse_all[None, :]).astype(jnp.bfloat16)
        else:
            owner_slots = neighbor_owner.T
            global_ids = owner_slots * node_dev + neighbor_row.T
            agg_one_cols = column_mean(node_features, global_ids, live.T, inverse_all)
    own_feats, own_agg_one = (
        lax.all_to_all(node_features, "mp", split_axis=1, concat_axis=0, tiled=True),
        lax.all_to_all(agg_one_cols, "mp", split_axis=1, concat_axis=0, tiled=True),
    )
    pre_one = contract(weights_one[:feat_width], own_feats, 0, 0) + contract(
        weights_one[feat_width:], own_agg_one, 0, 0
    )
    hidden_one = jax.nn.silu(pre_one).astype(jnp.bfloat16)
    with jax.named_scope("slot_tables"):
        blocks = has.reshape(devices * devices, node_dev).astype(jnp.bfloat16)
        before = (
            lax.broadcasted_iota(jnp.int32, (node_dev, node_dev), 0)
            < lax.broadcasted_iota(jnp.int32, (node_dev, node_dev), 1)
        ).astype(jnp.bfloat16)
        ranks = contract(blocks, before, 1, 0).astype(jnp.int32).reshape(devices, devices, node_dev)
        has_blocks = has.reshape(devices, devices, node_dev)
        rows_blocks = rowsel.reshape(devices, devices, node_dev)
        cap_ids = lax.broadcasted_iota(jnp.int32, (1, capacity, 1), 1)
        own_rank = lax.dynamic_index_in_dim(ranks, own_index, 1, keepdims=False)
        own_has = lax.dynamic_index_in_dim(has_blocks, own_index, 1, keepdims=False)
        gathered = ((own_rank[:, None, :] == cap_ids) & own_has[:, None, :]).astype(jnp.bfloat16)
        gathered = gathered.reshape(devices * capacity, node_dev)
        req_rank = lax.dynamic_index_in_dim(ranks, own_index, 0, keepdims=False)
        req_has = lax.dynamic_index_in_dim(has_blocks, own_index, 0, keepdims=False)
        req_rows = lax.dynamic_index_in_dim(rows_blocks, own_index, 0, keepdims=False)
        pick = ((req_rank[:, None, :] == cap_ids) & req_has[:, None, :]).astype(jnp.bfloat16)
        row_ids = lax.broadcasted_iota(jnp.int32, (1, 1, node_dev), 2)
        which = (req_rows[:, :, None] == row_ids).astype(jnp.bfloat16)
        asked = lax.dot_general(
            pick, which, (((2,), (1,)), ((0,), (0,))), preferred_element_type=jnp.float32
        )
        asked = asked.astype(jnp.bfloat16).reshape(devices * capacity, node_dev)
    own_inverse = lax.dynamic_slice_in_dim(inverse_all, own_index * node_dev, node_dev, 0)
    outgoing = contract(hidden_one, asked, 1, 1).astype(jnp.bfloat16)
    incoming = lax.all_to_all(outgoing, "mp", split_axis=1, concat_axis=1, tiled=True)
    total = contract(incoming, gathered, 1, 0)
    agg_two = (total * own_inverse[None, :]).astype(jnp.bfloat16)
    self_two = weights_two[:hidden]
    neigh_two = weights_two[hidden:]
    node_output = (
        contract(hidden_one, self_two, 0, 0) + contract(agg_two, neigh_two, 0, 0)
    ).astype(jnp.bfloat16)
    down_self = contract(self_two, cotangent, 1, 1)
    down_neigh = (contract(neigh_two, cotangent, 1, 1) * own_inverse[None, :]).astype(jnp.bfloat16)
    outgoing_grad = contract(down_neigh, gathered, 1, 1).astype(jnp.bfloat16)
    incoming_grad = lax.all_to_all(outgoing_grad, "mp", split_axis=1, concat_axis=1, tiled=True)
    neighbor_sum = contract(incoming_grad, asked, 1, 0)
    grad_hidden = down_self + neighbor_sum
    grad_pre = (grad_hidden * silu_slope(pre_one)).astype(jnp.bfloat16)
    terms = jnp.concatenate(
        [
            contract(own_feats, grad_pre, 1, 1),
            contract(own_agg_one, grad_pre, 1, 1),
            contract(hidden_one, cotangent, 1, 0),
            contract(agg_two, cotangent, 1, 0),
        ],
        axis=0,
    )
    weight_grads = lax.psum_scatter(terms, ("dp", "mp"), scatter_dimension=0, tiled=True)
    return (node_output, weight_grads)


def solution(mesh):
    in_specs = (
        P("mp", "dp"),
        P(),
        P(),
        P("dp", None),
        P("dp", None),
        P("dp"),
        P(("dp", "mp"), None),
    )
    out_specs = (P(("dp", "mp"), None), P(("dp", "mp"), None))
    return jax.shard_map(shards, mesh=mesh, in_specs=in_specs, out_specs=out_specs, check_vma=False)
```

profile of v0, /device:TPU:0, one launch (start us, length us, event | category | flops | bytes accessed | tf_op | source)
XLA Modules:
  0.0 325.1 jit_solution(16609977738096543799)
XLA Ops:
  7.2 1.3 all_to_all.40
  8.5 0.8 copy.27
  9.3 7.4 %all-to-all-start = ((bf16[32,16,192]{2,0,1:T(8,128)(2,1)}), bf16[32,16,192]{2,0,1:T(8,128)(2,1)S(1)}, u32[]{:S(2)}, u32[]{:S(2)}) async-start(bf16[32,16,192]{2,0,1:T(8,128)(2,1)} %copy.27), calls=%async_computation | async-start | bytes 524288 | tf_op jit(solution)/shard_map/all_to_all | solution.py:56
  16.7 0.7 iota_compare_fusion.9
  17.4 0.7 convert_divide_fusion
  18.2 1.8 select_reduce_fusion
  20.0 9.7 %bitcast_compare_fusion = pred[3072,3072]{1,0:T(32,128)(4,1)} fusion(s32[3072]{0:T(1024)S(1)} %eq.95, s32[16,3072]{1,0:T(8,128)S(1)} %select_reduce_fusion), kind=kLoop, calls=%fused_computation | loop fusion | flops 9437184 | bytes 9646080 | tf_op jit(solution)/shard_map/layer_one_mean/eq | solution.py:47
  29.9 8.5 %fusion.1 = bf16[32,3072]{1,0:T(8,128)(2,1)S(1)} fusion(pred[3072,3072]{1,0:T(32,128)(4,1)} %bitcast_compare_fusion, bf16[32,3072]{1,0:T(8,128)(2,1)S(1)} %copy-done.7, f32[3072]{0:T(1024)S(1)} %convert_divide_fusion), kind=kOutput, calls=%fused_computation.6 | convolution fusion | flops 604176384 | bytes 9842688 | tf_op jit(solution)/shard_map/layer_one_mean/dot_general | solution.py:22
  38.4 0.4 convolution_convert_fusion.2
  39.3 0.8 copy.28
  40.4 6.1 %all-to-all-start.1 = ((bf16[32,16,192]{2,0,1:T(8,128)(2,1)}), bf16[32,16,192]{2,0,1:T(8,128)(2,1)}, u32[]{:S(2)}, u32[]{:S(2)}) async-start(bf16[32,16,192]{2,0,1:T(8,128)(2,1)} %copy.28), calls=%async_computation.1 | async-start | bytes 524288 | tf_op jit(solution)/shard_map/all_to_all | solution.py:57
  46.7 0.5 fusion.8
  47.2 2.2 convolution_convert_fusion
  49.4 2.5 copy.31
  51.9 4.6 %all-to-all-done.1 = bf16[32,16,192]{2,0,1:T(8,128)(2,1)} async-done(((bf16[32,16,192]{2,0,1:T(8,128)(2,1)}), bf16[32,16,192]{2,0,1:T(8,128)(2,1)}, u32[]{:S(2)}, u32[]{:S(2)}) %all-to-all-start.1) | async-done | bytes 196640 | tf_op jit(solution)/shard_map/all_to_all | solution.py:57
  56.5 3.7 %all-to-all-start.3 = ((bf16[512,16,144]{0,2,1:T(8,128)(2,1)}), bf16[512,16,144]{0,2,1:T(8,128)(2,1)S(1)}, u32[]{:S(2)}, u32[]{:S(2)}) async-start(bf16[512,16,144]{0,2,1:T(8,128)(2,1)} %bitcast.16), calls=%async_computation.3 | async-start | bytes 4718592 | tf_op jit(solution)/shard_map/all_to_all | solution.py:100
  60.3 0.8 dynamic-slice_bitcast_fusion
  61.1 1.3 fusion.11
  62.8 1.3 fusion.18
  64.1 2.4 convolution_convert_fusion.1
  66.5 4.3 %copy.30 = bf16[512,2304]{0,1:T(8,128)(2,1)} copy(bf16[512,2304]{1,0:T(8,128)(2,1)} %convolution_convert_fusion.1) | data formatting | bytes 4718592 | tf_op jit(solution)/shard_map/convert_element_type | solution.py:88
  70.8 35.1 %all-to-all-done.3 = bf16[512,16,144]{0,2,1:T(8,128)(2,1)S(1)} async-done(((bf16[512,16,144]{0,2,1:T(8,128)(2,1)}), bf16[512,16,144]{0,2,1:T(8,128)(2,1)S(1)}, u32[]{:S(2)}, u32[]{:S(2)}) %all-to-all-start.3) | async-done | bytes 2359328 | tf_op jit(solution)/shard_map/all_to_all | solution.py:100
  105.9 12.3 %all-to-all-start.2 = ((bf16[512,16,144]{0,2,1:T(8,128)(2,1)}), bf16[512,16,144]{0,2,1:T(8,128)(2,1)}, u32[]{:S(2)}, u32[]{:S(2)}) async-start(bf16[512,16,144]{0,2,1:T(8,128)(2,1)} %bitcast.12), calls=%async_computation.2 | async-start | bytes 4718592 | tf_op jit(solution)/shard_map/all_to_all | solution.py:89
  118.2 1.4 fusion.42
  119.6 2.0 convolution_bitcast_fusion.1
  122.0 1.2 fusion.43
  123.5 40.4 %all-to-all-done.2 = bf16[512,16,144]{0,2,1:T(8,128)(2,1)} async-done(((bf16[512,16,144]{0,2,1:T(8,128)(2,1)}), bf16[512,16,144]{0,2,1:T(8,128)(2,1)}, u32[]{:S(2)}, u32[]{:S(2)}) %all-to-all-start.2) | async-done | bytes 2359328 | tf_op jit(solution)/shard_map/all_to_all | solution.py:89
  163.9 2.6 fusion.26
  166.9 2.4 pad_maximum_fusion
  169.3 1.2 copy-done.4
  170.8 1.0 fusion.30
  171.7 146.5 %reduce-scatter.2.cloned.1.call-done = f32[64,512]{1,0:T(8,128)} async-done(((f32[2048,512]{1,0:T(8,128)}), f32[64,512]{1,0:T(8,128)}) %reduce-scatter.2.cloned.1.call-update) | async-done | bytes 131088 | tf_op jit(solution)/shard_map/reduce_scatter | solution.py:113
  (41 shorter events, 2.8 us)
Async XLA Ops:
  7.2 40.0 %copy-start = (bf16[192,512]{1,0:T(8,128)(2,1)S(1)}, bf16[192,512]{1,0:T(8,128)(2,1)}, u32[]{:S(2)}) copy-start(bf16[192,512]{1,0:T(8,128)(2,1)} %param.13) | copy-start | bytes 589828
  9.3 31.1 %all-to-all-start = ((bf16[32,16,192]{2,0,1:T(8,128)(2,1)}), bf16[32,16,192]{2,0,1:T(8,128)(2,1)S(1)}, u32[]{:S(2)}, u32[]{:S(2)}) async-start(bf16[32,16,192]{2,0,1:T(8,128)(2,1)} %copy.27), calls=%async_computation | async-start | bytes 524288 | tf_op jit(solution)/shard_map/all_to_all | solution.py:56
  20.0 9.9 %copy-start.7 = (bf16[32,3072]{1,0:T(8,128)(2,1)S(1)}, bf16[32,3072]{1,0:T(8,128)(2,1)}, u32[]{:S(2)}) copy-start(bf16[32,3072]{1,0:T(8,128)(2,1)} %param.7) | copy-start | bytes 589828
  39.0 7.7 %copy-start.1 = (s32[16,16,192]{2,1,0:T(8,128)}, s32[16,16,192]{2,1,0:T(8,128)S(1)}, u32[]{:S(2)}) copy-start(s32[16,16,192]{2,1,0:T(8,128)S(1)} %reduce_max.12) | copy-start | bytes 589828
  40.2 6.4 %copy-start.6 = (s32[256,192]{1,0:T(8,128)}, s32[256,192]{1,0:T(8,128)S(1)}, u32[]{:S(2)}) copy-start(s32[256,192]{1,0:T(8,128)S(1)} %copy.29) | copy-start | bytes 589828
  40.4 16.2 %all-to-all-start.1 = ((bf16[32,16,192]{2,0,1:T(8,128)(2,1)}), bf16[32,16,192]{2,0,1:T(8,128)(2,1)}, u32[]{:S(2)}, u32[]{:S(2)}) async-start(bf16[32,16,192]{2,0,1:T(8,128)(2,1)} %copy.28), calls=%async_computation.1 | async-start | bytes 524288 | tf_op jit(solution)/shard_map/all_to_all | solution.py:57
  56.5 49.3 %all-to-all-start.3 = ((bf16[512,16,144]{0,2,1:T(8,128)(2,1)}), bf16[512,16,144]{0,2,1:T(8,128)(2,1)S(1)}, u32[]{:S(2)}, u32[]{:S(2)}) async-start(bf16[512,16,144]{0,2,1:T(8,128)(2,1)} %bitcast.16), calls=%async_computation.3 | async-start | bytes 4718592 | tf_op jit(solution)/shard_map/all_to_all | solution.py:100
  60.3 2.2 copy-start.2
  62.5 1.7 copy-start.8
  105.9 58.0 %all-to-all-start.2 = ((bf16[512,16,144]{0,2,1:T(8,128)(2,1)}), bf16[512,16,144]{0,2,1:T(8,128)(2,1)}, u32[]{:S(2)}, u32[]{:S(2)}) async-start(bf16[512,16,144]{0,2,1:T(8,128)(2,1)} %bitcast.12), calls=%async_computation.2 | async-start | bytes 4718592 | tf_op jit(solution)/shard_map/all_to_all | solution.py:89
  118.2 200.1 %reduce-scatter.2.cloned.1.call-start = ((), (), s32[]{:S(2)}) async-start(), calls=%async_computation.5 | async-start | bytes 4325376 | tf_op jit(solution)/shard_map/reduce_scatter | solution.py:113
  119.6 2.0 copy-start.3
  163.9 3.0 copy-start.5
  169.3 1.2 copy-start.4
Sparse Core Ops, SparseCore 0:
  169.4 148.7 reduce-scatter.1
where the time goes:
time: 326 us; the launch traced here: 325 us
  waiting for transfers between devices  227 us (70%)
  starting transfers between devices  29.5 us (9%)
  matrix products  25.9 us (8%)
  other arithmetic  15.9 us (5%)
  between operations  14.4 us (4%)
  local copies, waits for them, and re-layouts  12.7 us (4%)
    reduce_scatter x1, waiting for transfers between devices, shards(): lax.psum_scatter(terms, ('dp', 'mp'), scatter_dimension=0, tiled=True)  147 us
    all_to_all x1, waiting for transfers between devices, shards(): lax.all_to_all(outgoing, 'mp', split_axis=1, concat_axis=1, tiled=True)  40.4 us
    all_to_all x1, waiting for transfers between devices, shards(): lax.all_to_all(outgoing_grad, 'mp', split_axis=1, concat_axis=1, tiled=True)  35.1 us
    dot_general x15, matrix products, contract(): lax.dot_general(left, right, (((left_dim,), (right_dim,)), ((), ())), pre...  24.6 us
    all_to_all x1, starting transfers between devices, shards(): lax.all_to_all(outgoing, 'mp', split_axis=1, concat_axis=1, tiled=True)  12.3 us
    eq x1, other arithmetic, shards(): adjacency = (rowsel[:, None, :] == row_ids).astype(jnp.bfloat16)  9.7 us
    all_to_all x1, starting transfers between devices, shards(): lax.all_to_all(node_features, 'mp', split_axis=1, concat_axis=0, tiled=True)  7.39 us
  transfers between devices with their start and end apart: 5, of which 4 were waited for; matrix products, arithmetic and copies ran while one was open for 14% of the time, Pallas kernels for 0%

commit v1 on v0

--- a/solution.py
+++ b/solution.py
@@ -2,6 +2,21 @@
 import jax.numpy as jnp
 from jax import lax
 from jax.sharding import PartitionSpec as P
+from jax.lax import axis_index, axis_size, ppermute
+
+
+def produce_weights_on(target, d_out, matrix):
+    y_new = target.shape
+    front = target.reshape(*y_new[:d_out], matrix, y_new[d_out] // matrix, *y_new[d_out + 1 :])
+    b_next = jnp.moveaxis(front, d_out, 0)
+    return b_next
+
+
+def part_lanes(z, k_dim):
+    z = jnp.moveaxis(z, 0, k_dim)
+    a_now = z.shape
+    oldest = z.reshape(*a_now[:k_dim], a_now[k_dim] * a_now[k_dim + 1], *a_now[k_dim + 2 :])
+    return oldest
 
 
 def column_mean(table, indices, live, inverse):
@@ -86,7 +101,17 @@
         asked = asked.astype(jnp.bfloat16).reshape(devices * capacity, node_dev)
     own_inverse = lax.dynamic_slice_in_dim(inverse_all, own_index * node_dev, node_dev, 0)
     outgoing = contract(hidden_one, asked, 1, 1).astype(jnp.bfloat16)
-    incoming = lax.all_to_all(outgoing, "mp", split_axis=1, concat_axis=1, tiled=True)
+    res, frame_out = (axis_size("mp"), axis_index("mp"))
+    fresh = produce_weights_on(outgoing, 1, res)
+    to_i = 1
+    tall = fresh
+    while to_i < res:
+        w2, earlier = ((frame_out + to_i) % res, (frame_out - to_i) % res)
+        plain = lax.dynamic_index_in_dim(fresh, w2, 0)
+        e_next = ppermute(plain, "mp", [(jj, (jj + to_i) % res) for jj in range(res)])
+        tall = lax.dynamic_update_slice_in_dim(tall, e_next, earlier, axis=0)
+        to_i += 1
+    incoming = part_lanes(tall, 1)
     total = contract(incoming, gathered, 1, 0)
     agg_two = (total * own_inverse[None, :]).astype(jnp.bfloat16)
     self_two = weights_two[:hidden]

time: 326 us -> 327 us (level)
  starting transfers between devices: 29.5 us -> 62.4 us
  waiting for transfers between devices: 227 us -> 198 us
    ppermute x0 -> x15, waiting for transfers between devices: none -> 51.3 us  [shards(): ppermute(plain, 'mp', [(jj, (jj + to_i) % res) for jj in range(res)])]
    ppermute x0 -> x15, starting transfers between devices: none -> 44.5 us  [shards(): ppermute(plain, 'mp', [(jj, (jj + to_i) % res) for jj in range(res)])]
    all_to_all x1 -> x0, waiting for transfers between devices: 40.4 us -> none  [shards(): lax.all_to_all(outgoing, 'mp', split_axis=1, concat_axis=1, tiled=True)]
    all_to_all x1, waiting for transfers between devices: 35.1 us -> 0.01 us  [shards(): lax.all_to_all(outgoing_grad, 'mp', split_axis=1, concat_axis=1, tiled=True)]
    all_to_all x1 -> x0, starting transfers between devices: 12.3 us -> none  [shards(): lax.all_to_all(outgoing, 'mp', split_axis=1, concat_axis=1, tiled=True)]
    reduce_scatter x1, waiting for transfers between devices: 147 us -> 142 us  [shards(): lax.psum_scatter(terms, ('dp', 'mp'), scatter_dimension=0, tiled=True)]
  transfers between devices with their start and end apart: 5 -> 19, of which waited for: 4 -> 8; matrix products, arithmetic and copies ran while one was open for 14% -> 13% of each run, Pallas kernels for 0% -> 0%
where the time goes in v1:
time: 327 us
  waiting for transfers between devices  198 us (61%)
  starting transfers between devices  62.4 us (19%)
  matrix products  24.9 us (8%)
  other arithmetic  15.9 us (5%)
  between operations  15.2 us (5%)
  local copies, waits for them, and re-layouts  10.5 us (3%)
    reduce_scatter x1, waiting for transfers between devices, shards(): lax.psum_scatter(terms, ('dp', 'mp'), scatter_dimension=0, tiled=True)  142 us
    ppermute x15, waiting for transfers between devices, shards(): ppermute(plain, 'mp', [(jj, (jj + to_i) % res) for jj in range(res)])  51.3 us
    ppermute x15, starting transfers between devices, shards(): ppermute(plain, 'mp', [(jj, (jj + to_i) % res) for jj in range(res)])  44.5 us
    dot_general x15, matrix products, contract(): lax.dot_general(left, right, (((left_dim,), (right_dim,)), ((), ())), pre...  23.6 us
    eq x1, other arithmetic, shards(): adjacency = (rowsel[:, None, :] == row_ids).astype(jnp.bfloat16)  9.71 us
    all_to_all x1, starting transfers between devices, shards(): lax.all_to_all(node_features, 'mp', split_axis=1, concat_axis=0, tiled=True)  7.39 us
  transfers between devices with their start and end apart: 19, of which 8 were waited for; matrix products, arithmetic and copies ran while one was open for 13% of the time, Pallas kernels for 0%

profile of v1, /device:TPU:0, one launch (start us, length us, event | category | flops | bytes accessed | tf_op | source)
XLA Modules:
  0.0 326.6 jit_solution(10424123492674994331)
XLA Ops:
  7.2 1.3 all_to_all.34
  9.3 7.4 %all-to-all-start = ((bf16[32,16,192]{2,0,1:T(8,128)(2,1)}), bf16[32,16,192]{2,0,1:T(8,128)(2,1)S(1)}, u32[]{:S(2)}, u32[]{:S(2)}) async-start(bf16[32,16,192]{2,0,1:T(8,128)(2,1)} %copy.42), calls=%async_computation | async-start | bytes 524288 | tf_op jit(solution)/shard_map/all_to_all | solution.py:71
  18.2 1.8 select_reduce_fusion
  20.0 9.7 %bitcast_compare_fusion = pred[3072,3072]{1,0:T(32,128)(4,1)} fusion(s32[3072]{0:T(1024)S(1)} %eq.126, s32[16,3072]{1,0:T(8,128)S(1)} %select_reduce_fusion), kind=kLoop, calls=%fused_computation | loop fusion | flops 9437184 | bytes 9646080 | tf_op jit(solution)/shard_map/layer_one_mean/eq | solution.py:62
  29.9 8.5 %fusion.1 = bf16[32,3072]{1,0:T(8,128)(2,1)S(1)} fusion(pred[3072,3072]{1,0:T(32,128)(4,1)} %bitcast_compare_fusion, bf16[32,3072]{1,0:T(8,128)(2,1)S(1)} %copy-done.6, f32[3072]{0:T(1024)S(1)} %convert_divide_fusion), kind=kOutput, calls=%fused_computation.6 | convolution fusion | flops 604176384 | bytes 9842688 | tf_op jit(solution)/shard_map/layer_one_mean/dot_general | solution.py:37
  40.4 6.1 %all-to-all-start.1 = ((bf16[32,16,192]{2,0,1:T(8,128)(2,1)}), bf16[32,16,192]{2,0,1:T(8,128)(2,1)}, u32[]{:S(2)}, u32[]{:S(2)}) async-start(bf16[32,16,192]{2,0,1:T(8,128)(2,1)} %copy.43), calls=%async_computation.1 | async-start | bytes 524288 | tf_op jit(solution)/shard_map/all_to_all | solution.py:72
  47.2 2.2 convolution_convert_fusion
  49.4 2.5 copy.46
  51.9 4.6 %all-to-all-done.1 = bf16[32,16,192]{2,0,1:T(8,128)(2,1)} async-done(((bf16[32,16,192]{2,0,1:T(8,128)(2,1)}), bf16[32,16,192]{2,0,1:T(8,128)(2,1)}, u32[]{:S(2)}, u32[]{:S(2)}) %all-to-all-start.1) | async-done | bytes 196640 | tf_op jit(solution)/shard_map/all_to_all | solution.py:72
  56.6 4.4 %all-to-all-start.2 = ((bf16[512,16,144]{0,2,1:T(8,128)(2,1)}), bf16[512,16,144]{0,2,1:T(8,128)(2,1)}, u32[]{:S(2)}, u32[]{:S(2)}) async-start(bf16[512,16,144]{0,2,1:T(8,128)(2,1)} %bitcast.33), calls=%async_computation.2 | async-start | bytes 4718592 | tf_op jit(solution)/shard_map/all_to_all | solution.py:125
  62.5 1.3 fusion.12
  64.1 1.3 fusion.21
  65.5 2.4 convolution_convert_fusion.1
  67.8 2.8 copy.45
  71.2 1.7 collective-permute-start.1
  72.9 1.4 fusion.49
  74.2 2.2 collective-permute-start.2
  76.5 1.5 collective-permute-start.3
  78.1 29.5 %collective-permute-done = bf16[1,512,144]{1,2,0:T(8,128)(2,1)S(1)} collective-permute-done((bf16[1,512,144]{1,2,0:T(8,128)(2,1)S(1)}, bf16[1,512,144]{1,2,0:T(8,128)(2,1)S(1)}, u32[]{:S(2)}, u32[]{:S(2)}) %collective-permute-start) | collective-permute-done | bytes 147488 | tf_op jit(solution)/shard_map/ppermute | solution.py:111
  108.6 16.8 %collective-permute-start.6 = (bf16[1,512,144]{1,2,0:T(8,128)(2,1)S(1)}, bf16[1,512,144]{1,2,0:T(8,128)(2,1)S(1)}, u32[]{:S(2)}, u32[]{:S(2)}) collective-permute-start(bf16[1,512,144]{1,2,0:T(8,128)(2,1)S(1)} %get-tuple-element.10), channel_id=1, source_target_pairs={{0,7},{1,8},{2,9},{3,10},{4,11},{5,12},{6,13},{7,14},{8,15},{9,0},... | collective-permute-start | bytes 442376 | tf_op jit(solution)/shard_map/ppermute | solution.py:111
  125.5 2.5 collective-permute-start.8
  128.1 16.5 %collective-permute-done.4 = bf16[1,512,144]{1,2,0:T(8,128)(2,1)S(1)} collective-permute-done((bf16[1,512,144]{1,2,0:T(8,128)(2,1)S(1)}, bf16[1,512,144]{1,2,0:T(8,128)(2,1)S(1)}, u32[]{:S(2)}, u32[]{:S(2)}) %collective-permute-start.4) | collective-permute-done | bytes 147488 | tf_op jit(solution)/shard_map/ppermute | solution.py:111
  145.5 1.5 collective-permute-start.10
  147.0 7.7 %collective-permute-start.11 = (bf16[1,512,144]{1,2,0:T(8,128)(2,1)S(1)}, bf16[1,512,144]{1,2,0:T(8,128)(2,1)S(1)}, u32[]{:S(2)}, u32[]{:S(2)}) collective-permute-start(bf16[1,512,144]{1,2,0:T(8,128)(2,1)S(1)} %get-tuple-element.5), channel_id=1, source_target_pairs={{0,12},{1,13},{2,14},{3,15},{4,0},{5,1},{6,2},{7,3},{8,4},{9,5},{1... | collective-permute-start | bytes 442376 | tf_op jit(solution)/shard_map/ppermute | solution.py:111
  154.7 1.1 collective-permute-start.12
  155.8 5.3 %collective-permute-start.13 = (bf16[1,512,144]{1,2,0:T(8,128)(2,1)S(1)}, bf16[1,512,144]{1,2,0:T(8,128)(2,1)S(1)}, u32[]{:S(2)}, u32[]{:S(2)}) collective-permute-start(bf16[1,512,144]{1,2,0:T(8,128)(2,1)S(1)} %get-tuple-element.3), channel_id=1, source_target_pairs={{0,14},{1,15},{2,0},{3,1},{4,2},{5,3},{6,4},{7,5},{8,6},{9,7},{10,... | collective-permute-start | bytes 442376 | tf_op jit(solution)/shard_map/ppermute | solution.py:111
  161.1 3.7 %collective-permute-start.14 = (bf16[1,512,144]{1,2,0:T(8,128)(2,1)S(1)}, bf16[1,512,144]{1,2,0:T(8,128)(2,1)S(1)}, u32[]{:S(2)}, u32[]{:S(2)}) collective-permute-start(bf16[1,512,144]{1,2,0:T(8,128)(2,1)S(1)} %get-tuple-element.2), channel_id=1, source_target_pairs={{0,15},{1,0},{2,1},{3,2},{4,3},{5,4},{6,5},{7,6},{8,7},{9,8},{10,9... | collective-permute-start | bytes 442376 | tf_op jit(solution)/shard_map/ppermute | solution.py:111
  164.9 3.1 collective-permute-done.13
  169.6 2.7 convolution_bitcast_fusion.1
  172.8 1.2 fusion.50
  174.3 2.4 pad_maximum_fusion
  178.0 141.8 %reduce-scatter.2.cloned.1.call-done = f32[64,512]{1,0:T(8,128)} async-done(((f32[2048,512]{1,0:T(8,128)}), f32[64,512]{1,0:T(8,128)}) %reduce-scatter.2.cloned.1.call-update) | async-done | bytes 131088 | tf_op jit(solution)/shard_map/reduce_scatter | solution.py:138
  (83 shorter events, 12.5 us)
Async XLA Ops:
  7.2 40.0 %copy-start = (bf16[192,512]{1,0:T(8,128)(2,1)S(1)}, bf16[192,512]{1,0:T(8,128)(2,1)}, u32[]{:S(2)}) copy-start(bf16[192,512]{1,0:T(8,128)(2,1)} %param.13) | copy-start | bytes 589828
  9.3 31.1 %all-to-all-start = ((bf16[32,16,192]{2,0,1:T(8,128)(2,1)}), bf16[32,16,192]{2,0,1:T(8,128)(2,1)S(1)}, u32[]{:S(2)}, u32[]{:S(2)}) async-start(bf16[32,16,192]{2,0,1:T(8,128)(2,1)} %copy.42), calls=%async_computation | async-start | bytes 524288 | tf_op jit(solution)/shard_map/all_to_all | solution.py:71
  20.0 9.9 %copy-start.6 = (bf16[32,3072]{1,0:T(8,128)(2,1)S(1)}, bf16[32,3072]{1,0:T(8,128)(2,1)}, u32[]{:S(2)}) copy-start(bf16[32,3072]{1,0:T(8,128)(2,1)} %param.7) | copy-start | bytes 589828
  39.0 7.7 %copy-start.1 = (s32[16,16,192]{2,1,0:T(8,128)}, s32[16,16,192]{2,1,0:T(8,128)S(1)}, u32[]{:S(2)}) copy-start(s32[16,16,192]{2,1,0:T(8,128)S(1)} %reduce_max.12) | copy-start | bytes 589828
  40.3 6.4 %copy-start.5 = (s32[256,192]{1,0:T(8,128)}, s32[256,192]{1,0:T(8,128)S(1)}, u32[]{:S(2)}) copy-start(s32[256,192]{1,0:T(8,128)S(1)} %copy.44) | copy-start | bytes 589828
  40.4 16.2 %all-to-all-start.1 = ((bf16[32,16,192]{2,0,1:T(8,128)(2,1)}), bf16[32,16,192]{2,0,1:T(8,128)(2,1)}, u32[]{:S(2)}, u32[]{:S(2)}) async-start(bf16[32,16,192]{2,0,1:T(8,128)(2,1)} %copy.43), calls=%async_computation.1 | async-start | bytes 524288 | tf_op jit(solution)/shard_map/all_to_all | solution.py:72
  56.6 113.1 %all-to-all-start.2 = ((bf16[512,16,144]{0,2,1:T(8,128)(2,1)}), bf16[512,16,144]{0,2,1:T(8,128)(2,1)}, u32[]{:S(2)}, u32[]{:S(2)}) async-start(bf16[512,16,144]{0,2,1:T(8,128)(2,1)} %bitcast.33), calls=%async_computation.2 | async-start | bytes 4718592 | tf_op jit(solution)/shard_map/all_to_all | solution.py:125
  61.0 2.8 copy-start.2
  61.0 258.7 %reduce-scatter.2.cloned.1.call-start = ((), (), s32[]{:S(2)}) async-start(), calls=%async_computation.4 | async-start | bytes 4325376 | tf_op jit(solution)/shard_map/reduce_scatter | solution.py:138
  63.8 1.7 copy-start.7
  70.9 36.8 %collective-permute-start = (bf16[1,512,144]{1,2,0:T(8,128)(2,1)S(1)}, bf16[1,512,144]{1,2,0:T(8,128)(2,1)S(1)}, u32[]{:S(2)}, u32[]{:S(2)}) collective-permute-start(bf16[1,512,144]{1,2,0:T(8,128)(2,1)S(1)} %get-tuple-element.16), channel_id=1, source_target_pairs={{0,1},{1,2},{2,3},{3,4},{4,5},{5,6},{6,7},{7,8},{8,9},{9,10},{10,1... | collective-permute-start | bytes 442376 | tf_op jit(solution)/shard_map/ppermute | solution.py:111
  71.2 37.4 %collective-permute-start.1 = (bf16[1,512,144]{1,2,0:T(8,128)(2,1)S(1)}, bf16[1,512,144]{1,2,0:T(8,128)(2,1)S(1)}, u32[]{:S(2)}, u32[]{:S(2)}) collective-permute-start(bf16[1,512,144]{1,2,0:T(8,128)(2,1)S(1)} %get-tuple-element.15), channel_id=1, source_target_pairs={{0,2},{1,3},{2,4},{3,5},{4,6},{5,7},{6,8},{7,9},{8,10},{9,11},{10,... | collective-permute-start | bytes 442376 | tf_op jit(solution)/shard_map/ppermute | solution.py:111
  74.2 51.2 %collective-permute-start.2 = (bf16[1,512,144]{1,2,0:T(8,128)(2,1)S(1)}, bf16[1,512,144]{1,2,0:T(8,128)(2,1)S(1)}, u32[]{:S(2)}, u32[]{:S(2)}) collective-permute-start(bf16[1,512,144]{1,2,0:T(8,128)(2,1)S(1)} %get-tuple-element.14), channel_id=1, source_target_pairs={{0,3},{1,4},{2,5},{3,6},{4,7},{5,8},{6,9},{7,10},{8,11},{9,12},{10... | collective-permute-start | bytes 442376 | tf_op jit(solution)/shard_map/ppermute | solution.py:111
  76.5 49.0 %collective-permute-start.3 = (bf16[1,512,144]{1,2,0:T(8,128)(2,1)S(1)}, bf16[1,512,144]{1,2,0:T(8,128)(2,1)S(1)}, u32[]{:S(2)}, u32[]{:S(2)}) collective-permute-start(bf16[1,512,144]{1,2,0:T(8,128)(2,1)S(1)} %get-tuple-element.13), channel_id=1, source_target_pairs={{0,4},{1,5},{2,6},{3,7},{4,8},{5,9},{6,10},{7,11},{8,12},{9,13},{1... | collective-permute-start | bytes 442376 | tf_op jit(solution)/shard_map/ppermute | solution.py:111
  78.0 66.6 %collective-permute-start.4 = (bf16[1,512,144]{1,2,0:T(8,128)(2,1)S(1)}, bf16[1,512,144]{1,2,0:T(8,128)(2,1)S(1)}, u32[]{:S(2)}, u32[]{:S(2)}) collective-permute-start(bf16[1,512,144]{1,2,0:T(8,128)(2,1)S(1)} %get-tuple-element.12), channel_id=1, source_target_pairs={{0,5},{1,6},{2,7},{3,8},{4,9},{5,10},{6,11},{7,12},{8,13},{9,14},{... | collective-permute-start | bytes 442376 | tf_op jit(solution)/shard_map/ppermute | solution.py:111
  107.7 37.8 %collective-permute-start.5 = (bf16[1,512,144]{1,2,0:T(8,128)(2,1)S(1)}, bf16[1,512,144]{1,2,0:T(8,128)(2,1)S(1)}, u32[]{:S(2)}, u32[]{:S(2)}) collective-permute-start(bf16[1,512,144]{1,2,0:T(8,128)(2,1)S(1)} %get-tuple-element.11), channel_id=1, source_target_pairs={{0,6},{1,7},{2,8},{3,9},{4,10},{5,11},{6,12},{7,13},{8,14},{9,15},... | collective-permute-start | bytes 442376 | tf_op jit(solution)/shard_map/ppermute | solution.py:111
  108.6 38.4 %collective-permute-start.6 = (bf16[1,512,144]{1,2,0:T(8,128)(2,1)S(1)}, bf16[1,512,144]{1,2,0:T(8,128)(2,1)S(1)}, u32[]{:S(2)}, u32[]{:S(2)}) collective-permute-start(bf16[1,512,144]{1,2,0:T(8,128)(2,1)S(1)} %get-tuple-element.10), channel_id=1, source_target_pairs={{0,7},{1,8},{2,9},{3,10},{4,11},{5,12},{6,13},{7,14},{8,15},{9,0},... | collective-permute-start | bytes 442376 | tf_op jit(solution)/shard_map/ppermute | solution.py:111
  125.4 29.3 %collective-permute-start.7 = (bf16[1,512,144]{1,2,0:T(8,128)(2,1)S(1)}, bf16[1,512,144]{1,2,0:T(8,128)(2,1)S(1)}, u32[]{:S(2)}, u32[]{:S(2)}) collective-permute-start(bf16[1,512,144]{1,2,0:T(8,128)(2,1)S(1)} %get-tuple-element.9), channel_id=1, source_target_pairs={{0,8},{1,9},{2,10},{3,11},{4,12},{5,13},{6,14},{7,15},{8,0},{9,1},... | collective-permute-start | bytes 442376 | tf_op jit(solution)/shard_map/ppermute | solution.py:111
  125.5 30.3 %collective-permute-start.8 = (bf16[1,512,144]{1,2,0:T(8,128)(2,1)S(1)}, bf16[1,512,144]{1,2,0:T(8,128)(2,1)S(1)}, u32[]{:S(2)}, u32[]{:S(2)}) collective-permute-start(bf16[1,512,144]{1,2,0:T(8,128)(2,1)S(1)} %get-tuple-element.8), channel_id=1, source_target_pairs={{0,9},{1,10},{2,11},{3,12},{4,13},{5,14},{6,15},{7,0},{8,1},{9,2},... | collective-permute-start | bytes 442376 | tf_op jit(solution)/shard_map/ppermute | solution.py:111
  144.5 16.6 %collective-permute-start.9 = (bf16[1,512,144]{1,2,0:T(8,128)(2,1)S(1)}, bf16[1,512,144]{1,2,0:T(8,128)(2,1)S(1)}, u32[]{:S(2)}, u32[]{:S(2)}) collective-permute-start(bf16[1,512,144]{1,2,0:T(8,128)(2,1)S(1)} %get-tuple-element.7), channel_id=1, source_target_pairs={{0,10},{1,11},{2,12},{3,13},{4,14},{5,15},{6,0},{7,1},{8,2},{9,3},... | collective-permute-start | bytes 442376 | tf_op jit(solution)/shard_map/ppermute | solution.py:111
  145.5 19.4 %collective-permute-start.10 = (bf16[1,512,144]{1,2,0:T(8,128)(2,1)S(1)}, bf16[1,512,144]{1,2,0:T(8,128)(2,1)S(1)}, u32[]{:S(2)}, u32[]{:S(2)}) collective-permute-start(bf16[1,512,144]{1,2,0:T(8,128)(2,1)S(1)} %get-tuple-element.6), channel_id=1, source_target_pairs={{0,11},{1,12},{2,13},{3,14},{4,15},{5,0},{6,1},{7,2},{8,3},{9,4},{... | collective-permute-start | bytes 442376 | tf_op jit(solution)/shard_map/ppermute | solution.py:111
  147.0 17.9 %collective-permute-start.11 = (bf16[1,512,144]{1,2,0:T(8,128)(2,1)S(1)}, bf16[1,512,144]{1,2,0:T(8,128)(2,1)S(1)}, u32[]{:S(2)}, u32[]{:S(2)}) collective-permute-start(bf16[1,512,144]{1,2,0:T(8,128)(2,1)S(1)} %get-tuple-element.5), channel_id=1, source_target_pairs={{0,12},{1,13},{2,14},{3,15},{4,0},{5,1},{6,2},{7,3},{8,4},{9,5},{1... | collective-permute-start | bytes 442376 | tf_op jit(solution)/shard_map/ppermute | solution.py:111
  154.7 10.2 %collective-permute-start.12 = (bf16[1,512,144]{1,2,0:T(8,128)(2,1)S(1)}, bf16[1,512,144]{1,2,0:T(8,128)(2,1)S(1)}, u32[]{:S(2)}, u32[]{:S(2)}) collective-permute-start(bf16[1,512,144]{1,2,0:T(8,128)(2,1)S(1)} %get-tuple-element.4), channel_id=1, source_target_pairs={{0,13},{1,14},{2,15},{3,0},{4,1},{5,2},{6,3},{7,4},{8,5},{9,6},{10... | collective-permute-start | bytes 442376 | tf_op jit(solution)/shard_map/ppermute | solution.py:111
  155.8 12.2 %collective-permute-start.13 = (bf16[1,512,144]{1,2,0:T(8,128)(2,1)S(1)}, bf16[1,512,144]{1,2,0:T(8,128)(2,1)S(1)}, u32[]{:S(2)}, u32[]{:S(2)}) collective-permute-start(bf16[1,512,144]{1,2,0:T(8,128)(2,1)S(1)} %get-tuple-element.3), channel_id=1, source_target_pairs={{0,14},{1,15},{2,0},{3,1},{4,2},{5,3},{6,4},{7,5},{8,6},{9,7},{10,... | collective-permute-start | bytes 442376 | tf_op jit(solution)/shard_map/ppermute | solution.py:111
  161.1 7.2 %collective-permute-start.14 = (bf16[1,512,144]{1,2,0:T(8,128)(2,1)S(1)}, bf16[1,512,144]{1,2,0:T(8,128)(2,1)S(1)}, u32[]{:S(2)}, u32[]{:S(2)}) collective-permute-start(bf16[1,512,144]{1,2,0:T(8,128)(2,1)S(1)} %get-tuple-element.2), channel_id=1, source_target_pairs={{0,15},{1,0},{2,1},{3,2},{4,3},{5,4},{6,5},{7,6},{8,7},{9,8},{10,9... | collective-permute-start | bytes 442376 | tf_op jit(solution)/shard_map/ppermute | solution.py:111
  169.6 2.8 copy-start.3
  172.4 1.9 copy-start.4
Sparse Core Ops, SparseCore 0:
  176.8 142.8 reduce-scatter.1
